TPU v7x, 32 devices: a whole 2x2x4 slice. The times are simulated.
32 devices in a mesh: dp: 8 (over y, x, core), tensor: 4 (over z).
Axes of the slice: x: 2, y: 2, z: 4, core: 2. Of those that a mesh axis runs over, the one named last changes fastest.
Arguments:
- teacher_master: float32 [256, 16384], P('dp', 'tensor'), as said below
- student_weight: bfloat16 [256, 16384], P('dp', 'tensor'), may hold values from -6 to 6
- teacher_feat: bfloat16 [2048, 256], P('dp'), as said below
- student_feat: bfloat16 [2048, 256], P('dp'), may hold values from -6 to 6
- center: float32 [16384], P('tensor'), may hold values from -0.3 to 0.3
Outputs:
- master_new: float32 [256, 16384], P('dp', 'tensor')
- student_grad: float32 [256, 16384], P('dp', 'tensor')
- new_center: float32 [16384], P('tensor')
Inputs may be any that keep to these rules, and one draw needn't show every extreme that they name: `teacher_feat`: rows of teacher features are real-valued and of order one. `teacher_master`: entries of the teacher master are real-valued and of order one.
All inputs are finite; a program needn't handle non-finite values.
Results may differ from a plain program's by a relative error of at most 0.014.
Values may be sent and summed in bfloat16 or wider, within the bound.
No kernel may reach another device: no remote copies, remote signals or barrier semaphores. Data moves between devices by JAX's collectives and lax.ppermute only.
A program may use at most 64 MiB of HBM per device.

v0:
```python
import jax
import jax.numpy as jnp
from jax import lax
from jax.sharding import PartitionSpec as P


def unit_rows(feat):
    wide = feat.astype(jnp.float32)
    return (wide * lax.rsqrt(jnp.sum(wide * wide, 1, keepdims=True) + 1e-06)).astype(jnp.bfloat16)


def weight_plan(teacher_master, student_weight, teacher_feat, student_feat, center):
    zt = unit_rows(teacher_feat)
    zs = unit_rows(student_feat)
    images_all = teacher_feat.shape[0] * lax.axis_size("dp")
    student_full = lax.all_gather(student_weight, "dp", axis=0, tiled=True)
    master_new = 0.996 * teacher_master + 0.004 * student_weight.astype(jnp.float32)
    weight = lax.all_gather(master_new.astype(jnp.bfloat16), "dp", axis=0, tiled=True)
    raw = jnp.dot(zt, weight, preferred_element_type=jnp.float32)
    t_norm = jnp.sqrt(jnp.sum(jnp.square(weight.astype(jnp.float32)), 0) + 1e-06)
    t_cos = raw / t_norm
    s_norm = jnp.sqrt(jnp.sum(jnp.square(student_full.astype(jnp.float32)), 0) + 1e-06)
    s_cos = jnp.dot(zs, student_full, preferred_element_type=jnp.float32) / s_norm
    t_exp = jnp.exp((t_cos - center) / 0.04)
    s_exp = jnp.exp(s_cos / 0.1)
    t_total, s_total = lax.psum(
        (jnp.sum(t_exp, 1, keepdims=True), jnp.sum(s_exp, 1, keepdims=True)), "tensor"
    )
    cos_mean = lax.psum(jnp.sum(t_cos, 0), "dp") / images_all
    new_center = 0.5 * center + 0.5 * cos_mean
    dlog = ((s_exp / s_total - t_exp / t_total) / 0.1).astype(jnp.bfloat16)
    scaled = jnp.sum(dlog.astype(jnp.float32) * s_cos, 0) / s_norm
    product = lax.dot_general(
        zs, dlog, (((0,), (0,)), ((), ())), preferred_element_type=jnp.float32
    )
    student_grad = lax.psum_scatter(
        (product - student_full.astype(jnp.float32) * scaled) / s_norm,
        "dp",
        scatter_dimension=0,
        tiled=True,
    )
    return (master_new, student_grad, new_center)


def feature_plan(teacher_master, student_weight, teacher_feat, student_feat, center):
    ndp = lax.axis_size("dp")
    bot = teacher_feat.shape[1]
    images_all = teacher_feat.shape[0] * ndp
    cols = center.shape[0] // ndp
    master_new = 0.996 * teacher_master + 0.004 * student_weight.astype(jnp.float32)
    both = jnp.stack([student_weight, master_new.astype(jnp.bfloat16)])
    both = lax.all_to_all(both, "dp", 2, 1, tiled=True)
    sw, tw = (both[0], both[1])
    feats = jnp.concatenate([unit_rows(teacher_feat), unit_rows(student_feat)], axis=1)
    feats = lax.all_gather(feats, "dp", axis=0, tiled=True)
    zt, zs = (feats[:, :bot], feats[:, bot:])
    c = lax.dynamic_slice_in_dim(center, lax.axis_index("dp") * cols, cols)
    t_norm = jnp.sqrt(jnp.sum(jnp.square(tw.astype(jnp.float32)), 0) + 1e-06)
    s_norm = jnp.sqrt(jnp.sum(jnp.square(sw.astype(jnp.float32)), 0) + 1e-06)
    t_cos = jnp.dot(zt, tw, preferred_element_type=jnp.float32) / t_norm
    s_cos = jnp.dot(zs, sw, preferred_element_type=jnp.float32) / s_norm
    t_exp = jnp.exp((t_cos - c) / 0.04)
    s_exp = jnp.exp(s_cos / 0.1)
    totals = lax.psum(jnp.stack([jnp.sum(t_exp, 1), jnp.sum(s_exp, 1)], axis=1), ("dp", "tensor"))
    t_total, s_total = (totals[:, 0:1], totals[:, 1:2])
    part_center = 0.5 * c + 0.5 * (jnp.sum(t_cos, 0) / images_all)
    new_center = lax.all_gather(part_center, "dp", axis=0, tiled=True)
    dlog = ((s_exp / s_total - t_exp / t_total) / 0.1).astype(jnp.bfloat16)
    scaled = jnp.sum(dlog.astype(jnp.float32) * s_cos, 0) / s_norm
    product = lax.dot_general(
        zs, dlog, (((0,), (0,)), ((), ())), preferred_element_type=jnp.float32
    )
    grad = (product - sw.astype(jnp.float32) * scaled) / s_norm
    student_grad = lax.all_to_all(grad, "dp", 0, 1, tiled=True)
    return (master_new, student_grad, new_center)


def solution(mesh):
    placed = (P("dp", "tensor"), P("dp", "tensor"), P("dp", None), P("dp", None), P("tensor"))
    return jax.shard_map(
        shards_for(mesh),
        mesh=mesh,
        in_specs=placed,
        out_specs=(P("dp", "tensor"), P("dp", "tensor"), P("tensor")),
        check_vma=False,
    )


def shards_for(mesh):
    ndp = mesh.shape["dp"]

    def shards(teacher_master, student_weight, teacher_feat, student_feat, center):
        images_all = teacher_feat.shape[0] * ndp
        cols = center.shape[0]
        if images_all < cols and cols % ndp == 0:
            return feature_plan(teacher_master, student_weight, teacher_feat, student_feat, center)
        return weight_plan(teacher_master, student_weight, teacher_feat, student_feat, center)

    return shards
```

profile of v0, /device:TPU:0, one launch (start us, length us, event | category | flops | bytes accessed | tf_op | source)
XLA Modules:
  0.0 120.3 jit_solution(14048190160954956227)
XLA Ops:
  7.2 0.0 all-gather.3.cloned.1.call-start
  7.2 1.0 fusion.6
  8.2 1.0 fusion.8
  9.3 1.1 fusion.7
  10.4 0.7 pad_maximum_fusion.1
  11.1 0.0 all-gather.3.cloned.1.call-update
  11.1 2.0 %convert_bitcast_fusion = (bf16[1,32,4096]{2,1,0:T(8,128)(2,1)S(1)}, f32[32,4096]{1,0:T(8,128)}) fusion(bf16[32,4096]{1,0:T(8,128)(2,1)} %param.6, f32[32,4096]{1,0:T(8,128)} %param.5), kind=kLoop, calls=%fused_computation.26 | loop fusion | flops 655360 | bytes 1572864 | tf_op jit(solution)/shard_map/stack | solution.py:51
  13.1 1.0 pad_maximum_fusion
  14.1 2.8 %copy.18 = bf16[2,32,4096]{1,0,2:T(2,128)(2,1)S(1)} copy(bf16[2,32,4096]{2,1,0:T(8,128)(2,1)S(1)} %pad_maximum_fusion) | data formatting | bytes 1048576 | tf_op jit(solution)/shard_map/stack | solution.py:51
  16.9 2.7 %reshape.42 = bf16[8,2,16384]{2,1,0:T(2,128)(2,1)} reshape(bf16[4096,2,32]{2,1,0:T(2,128)(2,1)S(1)} %bitcast.22) | data formatting | bytes 1048576
  19.6 5.2 %all-to-all-start = ((bf16[8,2,16384]{2,1,0:T(2,128)(2,1)}), bf16[8,2,16384]{2,1,0:T(2,128)(2,1)S(1)}, u32[]{:S(2)}, u32[]{:S(2)}) async-start(bf16[8,2,16384]{2,1,0:T(2,128)(2,1)} %reshape.42), calls=%async_computation | async-start | bytes 1048576 | tf_op jit(solution)/shard_map/all_to_all | solution.py:52
  24.7 0.8 dynamic_slice.3
  25.5 9.0 %all-to-all-done = bf16[8,2,16384]{2,1,0:T(2,128)(2,1)S(1)} async-done(((bf16[8,2,16384]{2,1,0:T(2,128)(2,1)}), bf16[8,2,16384]{2,1,0:T(2,128)(2,1)S(1)}, u32[]{:S(2)}, u32[]{:S(2)}) %all-to-all-start) | async-done | bytes 524320 | tf_op jit(solution)/shard_map/all_to_all | solution.py:52
  34.5 1.0 reshape.43
  35.5 1.3 %copy.19 = bf16[2,32,8,512]{3,1,2,0:T(8,128)(2,1)S(1)} copy(bf16[2,32,8,512]{1,0,3,2:T(2,128)(2,1)S(1)} %bitcast.23) | data formatting | bytes 1048576 | tf_op jit(solution)/shard_map/all_to_all | solution.py:52
  36.9 0.1 multiply_reduce_fusion.1
  37.1 4.8 %all-gather.3.cloned.1.call-done = bf16[2048,512]{1,0:T(8,128)(2,1)} async-done(((bf16[256,512]{1,0:T(8,128)(2,1)}), bf16[2048,512]{1,0:T(8,128)(2,1)}) %all-gather.3.cloned.1.call-update) | async-done | bytes 2097168 | tf_op jit(solution)/shard_map/all_gather | solution.py:55
  41.9 0.0 copy-start
  41.9 4.1 %fusion = (f32[2048]{0:T(1024)S(1)}, f32[2048,512]{1,0:T(8,128)}) fusion(f32[512]{0:T(512)S(1)} %get-tuple-element.22, bf16[256,512]{1,0:T(8,128)(2,1)S(1)} %bitcast.29, bf16[2048,512]{1,0:T(8,128)(2,1)} %all-gather.3.cloned.1.call-done), kind=kOutput, calls=%fused_computation.4 | convolution fusion | flops 540014592 | bytes 5515264 | tf_op jit(solution)/shard_map/dot_general | solution.py:61
  46.0 0.0 copy-done
  46.0 3.1 %fusion.10 = (f32[512]{0:T(512)S(1)}, f32[2048]{0:T(1024)S(1)}, f32[2048,512]{1,0:T(8,128)}) fusion(f32[512]{0:T(512)S(1)} %dynamic_slice.3, f32[512]{0:T(512)S(1)} %get-tuple-element.21, bf16[256,512]{1,0:T(8,128)(2,1)S(1)} %bitcast.31, bf16[2048,512]{1,0:T(8,128)(2,1)S(1)} %copy-done), kind=kOutput, calls=%fused_computation.34 | convolution fusion | flops 542111232 | bytes 5519360 | tf_op jit(solution)/shard_map/dot_general | solution.py:60
  49.2 39.5 %psum.7 = f32[2048,2]{0,1:T(2,128)S(1)} all-reduce(f32[2048,2]{0,1:T(2,128)S(1)} %pad_maximum_fusion.2), channel_id=1, replica_groups=mesh['dp'=8,'tensor'=4] {'dp','tensor'}, use_global_device_ids=true, to_apply=%region_6.0 | all-reduce | flops 4096 | bytes 32768 | tf_op jit(solution)/shard_map/psum | solution.py:64
  88.7 4.5 %multiply_reduce_fusion = (f32[512]{0:T(512)S(1)}, bf16[2048,512]{1,0:T(8,128)(2,1)S(1)}) fusion(f32[2048,512]{1,0:T(8,128)} %get-tuple-element.19, f32[2048]{0:T(1024)S(1)} %bitcast.34, f32[2048,512]{1,0:T(8,128)} %get-tuple-element.20, f32[512]{0:T(512)S(1)} %dynamic_slice.3, f32[2048]{0:T(1024)S(1)} %bitcast.33), kind=kLoop, calls=%fused_computation | loop fusion | flops 11533824 | bytes 10506240 | tf_op jit(solution)/shard_map/reduce_sum | solution.py:69
  93.2 1.5 %fusion.2 = f32[256,512]{1,0:T(8,128)} fusion(bf16[2048,512]{1,0:T(8,128)(2,1)S(1)} %get-tuple-element.11, bf16[2048,512]{1,0:T(8,128)(2,1)S(1)} %copy-done, bf16[256,512]{1,0:T(8,128)(2,1)S(1)} %bitcast.30, f32[512]{0:T(512)S(1)} %get-tuple-element.22, f32[512]{0:T(512)S(1)} %rsqrt_multiply_fusion), kind=kOutput, calls=%fused_computation.9 | convolution fusion | flops 537395200 | bytes 3936256 | tf_op jit(solution)/shard_map/dot_general | solution.py:70
  94.8 4.4 %all-to-all-start.1 = ((f32[8,32,512]{2,1,0:T(8,128)}), f32[8,32,512]{2,1,0:T(8,128)S(1)}, u32[]{:S(2)}, u32[]{:S(2)}) async-start(f32[8,32,512]{2,1,0:T(8,128)} %bitcast.10), calls=%async_computation.1 | async-start | bytes 1048576 | tf_op jit(solution)/shard_map/all_to_all | solution.py:74
  99.2 0.8 multiply_add_fusion.1
  99.9 12.1 %all-gather = f32[8,1,512]{2,1,0:T(1,128)S(1)} all-gather(f32[1,1,512]{2,1,0:T(1,128)S(1)} %bitcast.35), channel_id=1, replica_groups=mesh['dp'=8,'tensor'=4] {'dp'}, dimensions={0}, use_global_device_ids=true | all-gather | bytes 18432 | tf_op jit(solution)/shard_map/all_gather | solution.py:67
  112.0 0.0 all-to-all-done.1
  112.0 0.8 copy.21
  112.8 0.6 copy.23
  (7 shorter events, 0.1 us)
Async XLA Ops:
  7.2 34.7 %all-gather.3.cloned.1.call-start = ((), (), s32[]{:S(2)}) async-start(), calls=%async_computation.2 | async-start | bytes 2359296 | tf_op jit(solution)/shard_map/all_gather | solution.py:55
  19.6 14.9 %all-to-all-start = ((bf16[8,2,16384]{2,1,0:T(2,128)(2,1)}), bf16[8,2,16384]{2,1,0:T(2,128)(2,1)S(1)}, u32[]{:S(2)}, u32[]{:S(2)}) async-start(bf16[8,2,16384]{2,1,0:T(2,128)(2,1)} %reshape.42), calls=%async_computation | async-start | bytes 1048576 | tf_op jit(solution)/shard_map/all_to_all | solution.py:52
  41.9 4.1 %copy-start = (bf16[2048,512]{1,0:T(8,128)(2,1)S(1)}, bf16[2048,512]{1,0:T(8,128)(2,1)}, u32[]{:S(2)}) copy-start(bf16[2048,512]{1,0:T(8,128)(2,1)} %all-gather.3.cloned.1.call-done) | copy-start | bytes 6291460
  94.8 17.2 %all-to-all-start.1 = ((f32[8,32,512]{2,1,0:T(8,128)}), f32[8,32,512]{2,1,0:T(8,128)S(1)}, u32[]{:S(2)}, u32[]{:S(2)}) async-start(f32[8,32,512]{2,1,0:T(8,128)} %bitcast.10), calls=%async_computation.1 | async-start | bytes 1048576 | tf_op jit(solution)/shard_map/all_to_all | solution.py:74
Sparse Core Ops, SparseCore 0:
  11.2 30.5 all-gather.2
where the time goes:
time: 121 us; the launch traced here: 120 us
  blocking collectives  51.6 us (43%)
  between operations  14.1 us (12%)
  waiting for transfers between devices  13.8 us (11%)
  other arithmetic  12.3 us (10%)
  local copies, waits for them, and re-layouts  10.1 us (8%)
  starting transfers between devices  9.6 us (8%)
  matrix products  8.79 us (7%)
    psum x1, blocking collectives, feature_plan(): lax.psum(jnp.stack([jnp.sum(t_exp, 1), jnp.sum(s_exp, 1)], axis=1), ('dp'...  39.5 us
    all_gather x1, blocking collectives, feature_plan(): new_center = lax.all_gather(part_center, 'dp', axis=0, tiled=True)  12.1 us
    all_to_all x1, waiting for transfers between devices, feature_plan(): both = lax.all_to_all(both, 'dp', 2, 1, tiled=True)  8.99 us
    all_to_all x1, starting transfers between devices, feature_plan(): both = lax.all_to_all(both, 'dp', 2, 1, tiled=True)  5.17 us
    all_gather x1, waiting for transfers between devices, feature_plan(): feats = lax.all_gather(feats, 'dp', axis=0, tiled=True)  4.81 us
    reduce_sum x1, other arithmetic, feature_plan(): scaled = jnp.sum(dlog.astype(jnp.float32) * s_cos, 0) / s_norm  4.52 us
    all_to_all x1, starting transfers between devices, feature_plan(): student_grad = lax.all_to_all(grad, 'dp', 0, 1, tiled=True)  4.39 us
    unnamed x5, local copies, waits for them, and re-layouts  4.31 us
  transfers between devices with their start and end apart: 3, of which 2 were waited for; matrix products, arithmetic and copies ran while one was open for 10% of the time, Pallas kernels for 0%

commit v1 on v0

--- a/solution.py
+++ b/solution.py
@@ -52,7 +52,15 @@
     both = lax.all_to_all(both, "dp", 2, 1, tiled=True)
     sw, tw = (both[0], both[1])
     feats = jnp.concatenate([unit_rows(teacher_feat), unit_rows(student_feat)], axis=1)
-    feats = lax.all_gather(feats, "dp", axis=0, tiled=True)
+    ndev = lax.axis_size("dp")
+    samples = [(ii, (ii + 1) % ndev) for ii in range(ndev)]
+    u_next = [None] * ndev
+    u_next[ndev - 1] = feats
+    for src_i in range(ndev - 2, -1, -1):
+        u_next[src_i] = lax.ppermute(u_next[src_i + 1], "dp", perm=samples)
+    v_next = jnp.concatenate(u_next, axis=0)
+    e_now = (lax.axis_index("dp") + 1) * feats.shape[0]
+    feats = jnp.roll(v_next, e_now, axis=0)
     zt, zs = (feats[:, :bot], feats[:, bot:])
     c = lax.dynamic_slice_in_dim(center, lax.axis_index("dp") * cols, cols)
     t_norm = jnp.sqrt(jnp.sum(jnp.square(tw.astype(jnp.float32)), 0) + 1e-06)

time: 121 us -> 143 us (1.18)
  waiting for transfers between devices: 13.8 us -> 41.2 us
  between operations: 14.1 us -> 0.84 us
  local copies, waits for them, and re-layouts: 10.1 us -> 17.9 us
    ppermute x0 -> x7, waiting for transfers between devices: none -> 41.2 us  [feature_plan(): u_next[src_i] = lax.ppermute(u_next[src_i + 1], 'dp', perm=samples)]
    all_to_all x1, waiting for transfers between devices: 8.99 us -> 0.01 us  [feature_plan(): both = lax.all_to_all(both, 'dp', 2, 1, tiled=True)]
    unnamed x5 -> x19, local copies, waits for them, and re-layouts: 4.31 us -> 12.2 us
    all_gather x1 -> x0, waiting for transfers between devices: 4.81 us -> none  [feature_plan(): feats = lax.all_gather(feats, 'dp', axis=0, tiled=True)]
  transfers between devices with their start and end apart: 3 -> 9, of which waited for: 2 -> 6; matrix products, arithmetic and copies ran while one was open for 10% -> 9% of each run, Pallas kernels for 0% -> 0%
where the time goes in v1:
time: 143 us; the launch traced here: 142 us
  blocking collectives  51.7 us (36%)
  waiting for transfers between devices  41.2 us (29%)
  local copies, waits for them, and re-layouts  17.9 us (13%)
  other arithmetic  11.6 us (8%)
  starting transfers between devices  9.69 us (7%)
  matrix products  9.08 us (6%)
    ppermute x7, waiting for transfers between devices, feature_plan(): u_next[src_i] = lax.ppermute(u_next[src_i + 1], 'dp', perm=samples)  41.2 us
    psum x1, blocking collectives, feature_plan(): lax.psum(jnp.stack([jnp.sum(t_exp, 1), jnp.sum(s_exp, 1)], axis=1), ('dp'...  39.7 us
    unnamed x19, local copies, waits for them, and re-layouts  12.2 us
    all_gather x1, blocking collectives, feature_plan(): new_center = lax.all_gather(part_center, 'dp', axis=0, tiled=True)  12.1 us
    all_to_all x1, starting transfers between devices, feature_plan(): both = lax.all_to_all(both, 'dp', 2, 1, tiled=True)  4.73 us
    reduce_sum x1, other arithmetic, feature_plan(): scaled = jnp.sum(dlog.astype(jnp.float32) * s_cos, 0) / s_norm  4.52 us
    all_to_all x1, starting transfers between devices, feature_plan(): student_grad = lax.all_to_all(grad, 'dp', 0, 1, tiled=True)  3.94 us
    dot_general x1, matrix products, feature_plan(): s_cos = jnp.dot(zs, sw, preferred_element_type=jnp.float32) / s_norm  3.21 us
  transfers between devices with their start and end apart: 9, of which 6 were waited for; matrix products, arithmetic and copies ran while one was open for 9% of the time, Pallas kernels for 0%

profile of v1, /device:TPU:0, one launch (start us, length us, event | category | flops | bytes accessed | tf_op | source)
XLA Modules:
  0.0 142.1 jit_solution(14228443467287470027)
XLA Ops:
  0.6 1.0 fusion.6
  1.7 1.0 fusion.8
  2.7 1.1 fusion.7
  3.8 0.5 collective-permute-start
  4.3 6.9 %collective-permute-done = bf16[256,512]{1,0:T(8,128)(2,1)S(1)} collective-permute-done((bf16[256,512]{1,0:T(8,128)(2,1)S(1)}, bf16[256,512]{1,0:T(8,128)(2,1)S(1)}, u32[]{:S(2)}, u32[]{:S(2)}) %collective-permute-start) | collective-permute-done | bytes 262176 | tf_op jit(solution)/shard_map/ppermute | solution.py:60
  11.3 0.0 collective-permute-start.1
  11.3 6.7 %collective-permute-done.1 = bf16[256,512]{1,0:T(8,128)(2,1)S(1)} collective-permute-done((bf16[256,512]{1,0:T(8,128)(2,1)S(1)}, bf16[256,512]{1,0:T(8,128)(2,1)S(1)}, u32[]{:S(2)}, u32[]{:S(2)}) %collective-permute-start.1) | collective-permute-done | bytes 262176 | tf_op jit(solution)/shard_map/ppermute | solution.py:60
  18.0 0.0 collective-permute-start.2
  18.0 2.0 %convert_bitcast_fusion = (bf16[1,32,4096]{2,1,0:T(8,128)(2,1)S(1)}, f32[32,4096]{1,0:T(8,128)}) fusion(bf16[32,4096]{1,0:T(8,128)(2,1)} %param.6, f32[32,4096]{1,0:T(8,128)} %param.5), kind=kLoop, calls=%fused_computation.26 | loop fusion | flops 655360 | bytes 1572864 | tf_op jit(solution)/shard_map/stack | solution.py:51
  20.0 4.8 %collective-permute-done.2 = bf16[256,512]{1,0:T(8,128)(2,1)} collective-permute-done((bf16[256,512]{1,0:T(8,128)(2,1)S(1)}, bf16[256,512]{1,0:T(8,128)(2,1)}, u32[]{:S(2)}, u32[]{:S(2)}) %collective-permute-start.2) | collective-permute-done | bytes 262176 | tf_op jit(solution)/shard_map/ppermute | solution.py:60
  24.8 0.0 collective-permute-start.3
  24.8 1.0 pad_maximum_fusion
  25.8 2.8 %copy.18 = bf16[2,32,4096]{1,0,2:T(2,128)(2,1)S(1)} copy(bf16[2,32,4096]{2,1,0:T(8,128)(2,1)S(1)} %pad_maximum_fusion) | data formatting | bytes 1048576 | tf_op jit(solution)/shard_map/stack | solution.py:51
  28.6 2.7 %reshape.42 = bf16[8,2,16384]{2,1,0:T(2,128)(2,1)} reshape(bf16[4096,2,32]{2,1,0:T(2,128)(2,1)S(1)} %bitcast.22) | data formatting | bytes 1048576
  31.2 4.7 %all-to-all-start = ((bf16[8,2,16384]{2,1,0:T(2,128)(2,1)}), bf16[8,2,16384]{2,1,0:T(2,128)(2,1)S(1)}, u32[]{:S(2)}, u32[]{:S(2)}) async-start(bf16[8,2,16384]{2,1,0:T(2,128)(2,1)} %reshape.42), calls=%async_computation | async-start | bytes 1048576 | tf_op jit(solution)/shard_map/all_to_all | solution.py:52
  36.0 0.0 collective-permute-done.3
  36.0 0.5 collective-permute-start.4
  36.5 12.1 %collective-permute-done.4 = bf16[256,512]{1,0:T(8,128)(2,1)} collective-permute-done((bf16[256,512]{1,0:T(8,128)(2,1)}, bf16[256,512]{1,0:T(8,128)(2,1)}, u32[]{:S(2)}, u32[]{:S(2)}) %collective-permute-start.4) | collective-permute-done | bytes 262176 | tf_op jit(solution)/shard_map/ppermute | solution.py:60
  48.6 0.0 collective-permute-start.5
  48.6 0.8 dynamic_slice.8
  49.4 0.0 all-to-all-done
  49.4 1.0 reshape.43
  50.4 1.3 copy.19
  51.7 0.1 multiply_reduce_fusion.1
  51.9 3.8 %collective-permute-done.5 = bf16[256,512]{1,0:T(8,128)(2,1)} collective-permute-done((bf16[256,512]{1,0:T(8,128)(2,1)}, bf16[256,512]{1,0:T(8,128)(2,1)}, u32[]{:S(2)}, u32[]{:S(2)}) %collective-permute-start.5) | collective-permute-done | bytes 262176 | tf_op jit(solution)/shard_map/ppermute | solution.py:60
  55.6 0.0 collective-permute-start.6
  55.7 6.8 %collective-permute-done.6 = bf16[256,512]{1,0:T(8,128)(2,1)S(1)} collective-permute-done((bf16[256,512]{1,0:T(8,128)(2,1)}, bf16[256,512]{1,0:T(8,128)(2,1)S(1)}, u32[]{:S(2)}, u32[]{:S(2)}) %collective-permute-start.6) | collective-permute-done | bytes 262176 | tf_op jit(solution)/shard_map/ppermute | solution.py:60
  62.6 1.0 constant_dynamic-update-slice_fusion.14
  63.5 1.0 constant_dynamic-update-slice_fusion.13
  64.5 1.0 constant_dynamic-update-slice_fusion.12
  65.5 1.0 constant_dynamic-update-slice_fusion.11
  66.6 1.0 constant_dynamic-update-slice_fusion.6
  67.5 1.0 constant_dynamic-update-slice_fusion.5
  68.5 1.0 constant_dynamic-update-slice_fusion.4
  69.5 1.0 constant_dynamic-update-slice_fusion.3
  70.5 0.0 copy-start
  70.5 3.2 %fusion = (f32[2048]{0:T(1024)S(1)}, f32[2048,512]{1,0:T(8,128)}) fusion(f32[512]{0:T(512)S(1)} %get-tuple-element.22, bf16[256,512]{1,0:T(8,128)(2,1)S(1)} %bitcast.29, bf16[4096,512]{1,0:T(8,128)(2,1)S(1)} %constant_dynamic-update-slice_fusion, s32[]{:T(128)S(6)} %select_n.17, s32[]{:T(128)S(6)} %add.67), kind=kOutput, calls=%fused_computation.4 | convolution fusion | flops 540014592 | bytes 5515272 | tf_op jit(solution)/shard_map/dot_general | solution.py:69
  73.8 0.0 copy-done
  73.8 3.1 %fusion.11 = (f32[512]{0:T(512)S(1)}, f32[2048]{0:T(1024)S(1)}, f32[2048,512]{1,0:T(8,128)}) fusion(f32[512]{0:T(512)S(1)} %dynamic_slice.8, f32[512]{0:T(512)S(1)} %get-tuple-element.21, bf16[256,512]{1,0:T(8,128)(2,1)S(1)} %bitcast.31, bf16[4096,512]{1,0:T(8,128)(2,1)S(1)} %constant_dynamic-update-slice_fusion, s32[]{:T(128)S(6)} %select_n.17), kind=kOutput, calls=%fused_computation.51 | convolution fusion | flops 542111232 | bytes 5519364 | tf_op jit(solution)/shard_map/dot_general | solution.py:68
  76.9 39.7 %psum.7 = f32[2048,2]{0,1:T(2,128)S(1)} all-reduce(f32[2048,2]{0,1:T(2,128)S(1)} %pad_maximum_fusion.2), channel_id=1, replica_groups=mesh['dp'=8,'tensor'=4] {'dp','tensor'}, use_global_device_ids=true, to_apply=%region_6.7 | all-reduce | flops 4096 | bytes 32768 | tf_op jit(solution)/shard_map/psum | solution.py:72
  116.6 4.5 %multiply_reduce_fusion = (f32[512]{0:T(512)S(1)}, bf16[2048,512]{1,0:T(8,128)(2,1)S(1)}) fusion(f32[2048,512]{1,0:T(8,128)} %get-tuple-element.19, f32[2048]{0:T(1024)S(1)} %bitcast.34, f32[2048,512]{1,0:T(8,128)} %get-tuple-element.20, f32[512]{0:T(512)S(1)} %dynamic_slice.8, f32[2048]{0:T(1024)S(1)} %bitcast.33), kind=kLoop, calls=%fused_computation | loop fusion | flops 11533824 | bytes 10506240 | tf_op jit(solution)/shard_map/reduce_sum | solution.py:77
  121.1 2.8 %fusion.2 = f32[256,512]{1,0:T(8,128)} fusion(bf16[2048,512]{1,0:T(8,128)(2,1)S(1)} %get-tuple-element.11, bf16[4096,512]{1,0:T(8,128)(2,1)} %copy-done, s32[]{:T(128)S(6)} %select_n.17, s32[]{:T(128)S(6)} %add.67, bf16[256,512]{1,0:T(8,128)(2,1)S(1)} %bitcast.30, f32[512]{0:T(512)S(1)} %get-tuple-element.22, f32[512]{0:T(512)S(1)} %rsqrt_multiply_fusion), kind=kOutput, calls=%fused_computation.9 | convolution fusion | flops 537395200 | bytes 3936264 | tf_op jit(solution)/shard_map/dot_general | solution.py:78
  123.9 3.9 %all-to-all-start.1 = ((f32[8,32,512]{2,1,0:T(8,128)}), f32[8,32,512]{2,1,0:T(8,128)S(1)}, u32[]{:S(2)}, u32[]{:S(2)}) async-start(f32[8,32,512]{2,1,0:T(8,128)} %bitcast.10), calls=%async_computation.1 | async-start | bytes 1048576 | tf_op jit(solution)/shard_map/all_to_all | solution.py:82
  127.8 0.8 multiply_add_fusion.1
  128.6 12.1 %all-gather = f32[8,1,512]{2,1,0:T(1,128)S(1)} all-gather(f32[1,1,512]{2,1,0:T(1,128)S(1)} %bitcast.35), channel_id=1, replica_groups=mesh['dp'=8,'tensor'=4] {'dp'}, dimensions={0}, use_global_device_ids=true | all-gather | bytes 18432 | tf_op jit(solution)/shard_map/all_gather | solution.py:75
  140.6 0.0 all-to-all-done.1
  140.6 0.8 copy.21
  141.5 0.6 copy.38
  (16 shorter events, 0.3 us)
Async XLA Ops:
  3.8 7.4 %collective-permute-start = (bf16[256,512]{1,0:T(8,128)(2,1)S(1)}, bf16[256,512]{1,0:T(8,128)(2,1)S(1)}, u32[]{:S(2)}, u32[]{:S(2)}) collective-permute-start(bf16[256,512]{1,0:T(8,128)(2,1)S(1)} %pad_maximum_fusion.1), channel_id=1, source_target_pairs={{0,4},{4,8},{8,12},{12,16},{16,20},{20,24},{24,28},{28,0},{1,5},{5... | collective-permute-start | bytes 786440 | tf_op jit(solution)/shard_map/ppermute | solution.py:60
  11.3 6.7 %collective-permute-start.1 = (bf16[256,512]{1,0:T(8,128)(2,1)S(1)}, bf16[256,512]{1,0:T(8,128)(2,1)S(1)}, u32[]{:S(2)}, u32[]{:S(2)}) collective-permute-start(bf16[256,512]{1,0:T(8,128)(2,1)S(1)} %collective-permute-done), channel_id=1, source_target_pairs={{0,4},{4,8},{8,12},{12,16},{16,20},{20,24},{24,28},{28,0},{1,5},{5... | collective-permute-start | bytes 786440 | tf_op jit(solution)/shard_map/ppermute | solution.py:60
  18.0 6.8 %collective-permute-start.2 = (bf16[256,512]{1,0:T(8,128)(2,1)S(1)}, bf16[256,512]{1,0:T(8,128)(2,1)}, u32[]{:S(2)}, u32[]{:S(2)}) collective-permute-start(bf16[256,512]{1,0:T(8,128)(2,1)S(1)} %collective-permute-done.1), channel_id=1, source_target_pairs={{0,4},{4,8},{8,12},{12,16},{16,20},{20,24},{24,28},{28,0},{1,5},{5... | collective-permute-start | bytes 786440 | tf_op jit(solution)/shard_map/ppermute | solution.py:60
  24.8 11.2 %collective-permute-start.3 = (bf16[256,512]{1,0:T(8,128)(2,1)}, bf16[256,512]{1,0:T(8,128)(2,1)}, u32[]{:S(2)}, u32[]{:S(2)}) collective-permute-start(bf16[256,512]{1,0:T(8,128)(2,1)} %collective-permute-done.2), channel_id=1, source_target_pairs={{0,4},{4,8},{8,12},{12,16},{16,20},{20,24},{24,28},{28,0},{1,5},{5... | collective-permute-start | bytes 786440 | tf_op jit(solution)/shard_map/ppermute | solution.py:60
  31.2 18.2 %all-to-all-start = ((bf16[8,2,16384]{2,1,0:T(2,128)(2,1)}), bf16[8,2,16384]{2,1,0:T(2,128)(2,1)S(1)}, u32[]{:S(2)}, u32[]{:S(2)}) async-start(bf16[8,2,16384]{2,1,0:T(2,128)(2,1)} %reshape.42), calls=%async_computation | async-start | bytes 1048576 | tf_op jit(solution)/shard_map/all_to_all | solution.py:52
  36.0 12.7 %collective-permute-start.4 = (bf16[256,512]{1,0:T(8,128)(2,1)}, bf16[256,512]{1,0:T(8,128)(2,1)}, u32[]{:S(2)}, u32[]{:S(2)}) collective-permute-start(bf16[256,512]{1,0:T(8,128)(2,1)} %collective-permute-done.3), channel_id=1, source_target_pairs={{0,4},{4,8},{8,12},{12,16},{16,20},{20,24},{24,28},{28,0},{1,5},{5... | collective-permute-start | bytes 786440 | tf_op jit(solution)/shard_map/ppermute | solution.py:60
  48.6 7.0 %collective-permute-start.5 = (bf16[256,512]{1,0:T(8,128)(2,1)}, bf16[256,512]{1,0:T(8,128)(2,1)}, u32[]{:S(2)}, u32[]{:S(2)}) collective-permute-start(bf16[256,512]{1,0:T(8,128)(2,1)} %collective-permute-done.4), channel_id=1, source_target_pairs={{0,4},{4,8},{8,12},{12,16},{16,20},{20,24},{24,28},{28,0},{1,5},{5... | collective-permute-start | bytes 786440 | tf_op jit(solution)/shard_map/ppermute | solution.py:60
  55.6 6.9 %collective-permute-start.6 = (bf16[256,512]{1,0:T(8,128)(2,1)}, bf16[256,512]{1,0:T(8,128)(2,1)S(1)}, u32[]{:S(2)}, u32[]{:S(2)}) collective-permute-start(bf16[256,512]{1,0:T(8,128)(2,1)} %collective-permute-done.5), channel_id=1, source_target_pairs={{0,4},{4,8},{8,12},{12,16},{16,20},{20,24},{24,28},{28,0},{1,5},{5... | collective-permute-start | bytes 786440 | tf_op jit(solution)/shard_map/ppermute | solution.py:60
  70.5 3.2 %copy-start = (bf16[4096,512]{1,0:T(8,128)(2,1)}, bf16[4096,512]{1,0:T(8,128)(2,1)S(1)}, u32[]{:S(2)}) copy-start(bf16[4096,512]{1,0:T(8,128)(2,1)S(1)} %constant_dynamic-update-slice_fusion) | copy-start | bytes 12582916
  123.9 16.8 %all-to-all-start.1 = ((f32[8,32,512]{2,1,0:T(8,128)}), f32[8,32,512]{2,1,0:T(8,128)S(1)}, u32[]{:S(2)}, u32[]{:S(2)}) async-start(f32[8,32,512]{2,1,0:T(8,128)} %bitcast.10), calls=%async_computation.1 | async-start | bytes 1048576 | tf_op jit(solution)/shard_map/all_to_all | solution.py:82
